TPU v7x, 256 devices: a whole 4x4x8 slice. The times are simulated.
256 devices in a mesh: dp: 4 (over x_lo, core), expert: 64 (over z, y, x_hi).
Axes of the slice: x: 4 (x_hi: 2, x_lo: 2; x = x_hi * 2 + x_lo), y: 4, z: 8, core: 2. Of those that a mesh axis runs over, the one named last changes fastest.
Arguments:
- prev_acts: bfloat16 [4, 64, 128, 3584], P('dp', 'expert'), may hold values from -6 to 6
- prev_cot: bfloat16 [4, 64, 128, 512], P('dp', 'expert'), may hold values from -0.59765625 to 0.59765625
- weights: bfloat16 [64, 3584, 512], P('expert', 'dp'), may hold values from -0.09375 to 0.09375
- first_moment: float32 [64, 3584, 512], P('expert', 'dp'), may hold values from -1.8 to 1.8
- second_moment: float32 [64, 3584, 512], P('expert', 'dp'), may hold values from 0.1 to 2
- tokens: bfloat16 [4, 64, 128, 3584], P('dp', 'expert'), may hold values from -6 to 6
- routing: int32 [4, 64, 128, 2], P('dp', 'expert'), may hold values from 0 to 15, all different within a row; in each aligned block of 128 rows (0 to 127, 128 to 255, ..., all dimensions but the last counted through in order) at most 24 rows name the same one
- gates: bfloat16 [4, 64, 128, 2], P('dp', 'expert'), may hold values from 0.19921875 to 1
- token_counts: int32 [4, 64], P('dp', 'expert'), may hold values from 64 to 128
- old_owner: int32 [16], replicated, may hold values from 0 to 15, each once
- new_owner: int32 [16], replicated, may hold values from 0 to 15, each once
Outputs:
- expert_hidden: bfloat16 [4, 64, 1536, 256], P('dp', 'expert')
- new_weights: bfloat16 [64, 3584, 512], P('expert', 'dp')
- new_first: float32 [64, 3584, 512], P('expert', 'dp')
- new_second: float32 [64, 3584, 512], P('expert', 'dp')
Inputs may be any that keep to these rules, and one draw needn't show every extreme that they name: `routing`: each token names 2 different hot experts; within the rows of one device no hot expert is named by more than 24 rows. `old_owner`: each is a permutation of the 16 groups. `new_owner`: each is a permutation of the 16 groups.
All inputs are finite; a program needn't handle non-finite values.
Results may differ from a plain program's by a relative error of at most 0.013.
Values may be sent and summed in bfloat16 or wider, within the bound.
No kernel may reach another device: no remote copies, remote signals or barrier semaphores. Data moves between devices by JAX's collectives and lax.ppermute only.
A program may use at most 128 MiB of HBM per device.

v0:
```python
import jax
import jax.numpy as jnp
from jax import lax
from jax.sharding import Mesh
from jax.sharding import PartitionSpec as P

D = 3584
GRP = 4
SCALE_PAD = 128
beta_first = 0.9
beta_second = 0.95
learning = 0.00022
decay_rate = 0.1
epsilon = 1e-08
first_fix = 1.0 - 0.9**40
second_fix = 1.0 - 0.95**40


def adamw(weight_now, first_now, second_now, gradient):
    first_next = beta_first * first_now + (1.0 - beta_first) * gradient
    second_next = beta_second * second_now + (1.0 - beta_second) * gradient * gradient
    stepped = weight_now.astype(jnp.float32) * (1.0 - learning * decay_rate) - learning * (
        first_next / first_fix
    ) / (jnp.sqrt(second_next / second_fix) + epsilon)
    return (stepped.astype(jnp.bfloat16), first_next, second_next)


def migrate(state, group_source, groups, mode=None):
    layers, rows_dev, width = state.shape
    piece_rows = rows_dev // groups
    split = state.reshape(layers, groups, piece_rows, width)
    spread = lax.all_to_all(split, "grp", split_axis=1, concat_axis=1, tiled=True)
    chosen = jnp.take(spread, group_source, axis=1, mode=mode)
    home = lax.all_to_all(chosen, "grp", split_axis=1, concat_axis=1, tiled=True)
    return home.reshape(layers, rows_dev, width)


def pack_tokens(token_block, route_block, gate_block, limit, hot_index, capacity):
    valid = jnp.arange(token_block.shape[0], dtype=jnp.int32) < limit
    hits = (route_block[:, :, None] == hot_index[None, None, :]) & valid[:, None, None]
    named = jnp.sum(hits.astype(jnp.int32), axis=1)
    scales = jnp.sum(jnp.where(hits, gate_block.astype(jnp.float32)[:, :, None], 0.0), axis=1)
    ranks = jnp.cumsum(named, axis=0) - named
    slots = jnp.arange(capacity, dtype=jnp.int32)
    placed = (ranks.T[:, None, :] == slots[None, :, None]) & (named.T[:, None, :] == 1)
    packed = jnp.einsum(
        "hct,td->hcd", placed.astype(jnp.bfloat16), token_block, preferred_element_type=jnp.float32
    ).astype(jnp.bfloat16)
    gate_scale = jnp.einsum("hct,th->hc", placed.astype(jnp.float32), scales).astype(jnp.bfloat16)
    return (packed, gate_scale)


def local(
    prev_acts,
    prev_cot,
    weights,
    first_moment,
    second_moment,
    tokens,
    routing,
    gates,
    token_counts,
    old_owner,
    new_owner,
):
    groups = lax.axis_size("grp")
    experts = groups * GRP
    token_slots = tokens.shape[2]
    capacity = min(token_slots, 3 * token_slots // groups)
    width = weights.shape[2]
    hidden_units = width // 2
    activations = prev_acts[0, 0]
    cotangent = prev_cot[0, 0]
    hot_index = jnp.arange(groups, dtype=jnp.int32)
    holder = jnp.sum(
        jnp.where(new_owner[None, :] == hot_index[:, None], hot_index[None, :], 0), axis=1
    )
    group_source = jnp.take(old_owner, holder)
    packed, gate_scale = pack_tokens(
        tokens[0, 0], routing[0, 0], gates[0, 0], token_counts[0, 0], holder, capacity
    )
    scale_cols = jnp.zeros((groups, capacity, SCALE_PAD), jnp.bfloat16).at[:, :, 0].set(gate_scale)
    payload = jnp.concatenate([packed, scale_cols], axis=2)
    by_group = lax.all_to_all(payload, "grp", split_axis=0, concat_axis=0, tiled=True)
    grads = lax.psum_scatter(
        lax.dot_general(
            activations, cotangent, (((0,), (0,)), ((), ())), preferred_element_type=jnp.float32
        ).astype(jnp.bfloat16),
        "dp",
        scatter_dimension=0,
        tiled=True,
    )
    by_group, grads = lax.optimization_barrier((by_group, grads))
    grads = grads.astype(jnp.float32)
    near = lax.all_gather(by_group, "ylo", axis=0, tiled=False)
    near = near.reshape(2 * groups * capacity, D + SCALE_PAD)
    stepped, first_next, second_next = adamw(weights[0], first_moment[0], second_moment[0], grads)
    weight_home = migrate(stepped[None], group_source, groups)
    new_weight = weight_home[0]
    moments = jnp.stack([first_next.astype(jnp.bfloat16), second_next.astype(jnp.bfloat16)])
    moments, new_weight = lax.optimization_barrier((moments, new_weight))
    moved = migrate(moments, group_source, groups, mode="clip")
    both = lax.all_gather(new_weight, ("xhi", "dp"), axis=0, tiled=True)
    both = both.reshape(2, -1, width)
    both = jnp.pad(both, ((0, 0), (0, SCALE_PAD), (0, 0)))
    projected = jnp.stack(
        [jnp.dot(near, both[k], preferred_element_type=jnp.float32) for k in range(2)]
    )
    scaling = near[:, D].astype(jnp.float32)
    result = (
        jax.nn.silu(projected[:, :, :hidden_units])
        * projected[:, :, hidden_units:]
        * scaling[None, :, None]
    ).astype(jnp.bfloat16)
    xhi = lax.axis_index("xhi")
    own = lax.dynamic_index_in_dim(result, xhi, axis=0, keepdims=False)
    other = lax.dynamic_index_in_dim(result, 1 - xhi, axis=0, keepdims=False)
    for_partner = lax.ppermute(other, "xhi", perm=[(0, 1), (1, 0)])
    mine = jnp.where(
        xhi == 0, jnp.stack([own, for_partner]), jnp.stack([for_partner, own])
    ).reshape(2, 2, groups, capacity, hidden_units)
    hidden = jnp.transpose(mine, (2, 1, 0, 3, 4)).reshape(1, 1, experts * capacity, hidden_units)
    return (
        hidden,
        weight_home,
        moved[0].astype(jnp.float32)[None],
        moved[1].astype(jnp.float32)[None],
    )


def solution(mesh):
    n_dp = mesh.shape["dp"]
    n_expert = mesh.shape["expert"]
    mesh4 = Mesh(mesh.devices.reshape(n_dp, n_expert // GRP, 2, 2), ("dp", "grp", "ylo", "xhi"))
    ex = ("grp", "ylo", "xhi")
    in_specs = (
        P("dp", ex, None, None),
        P("dp", ex, None, None),
        P(ex, "dp", None),
        P(ex, "dp", None),
        P(ex, "dp", None),
        P("dp", ex, None, None),
        P("dp", ex, None, None),
        P("dp", ex, None, None),
        P("dp", ex),
        P(),
        P(),
    )
    out_specs = (P("dp", ex, None, None), P(ex, "dp", None), P(ex, "dp", None), P(ex, "dp", None))
    return jax.shard_map(local, mesh=mesh4, in_specs=in_specs, out_specs=out_specs, check_vma=False)
```

profile of v0, /device:TPU:6, one launch (start us, length us, event | category | flops | bytes accessed | tf_op | source)
XLA Modules:
  0.0 284.6 jit_solution(10818399610023016619)
XLA Ops:
  7.2 0.0 copy-start
  7.2 0.0 reduce-scatter.2.cloned.1.call-start
  7.2 1.1 copy-done
  8.3 3.8 %convolution_convert_fusion = bf16[3584,512]{1,0:T(8,128)(2,1)} fusion(bf16[1,1,128,3584]{3,2,1,0:T(8,128)(2,1)S(1)} %copy-done, bf16[1,1,128,512]{3,2,1,0:T(8,128)(2,1)} %param.14), kind=kOutput, calls=%fused_computation.5 | convolution fusion | flops 471597056 | bytes 4718592 | tf_op jit(solution)/shard_map/dot_general | solution.py:86
  12.2 0.0 copy-start.9
  12.2 0.0 copy-start.7
  12.2 0.0 copy-start.10
  12.2 0.0 reduce-scatter.2.cloned.1.call-update
  12.2 0.0 all-gather.6.cloned.1.call-start
  12.3 0.6 copy-done.9
  12.8 0.1 select_reduce_fusion.1
  13.6 0.0 copy-done.7
  13.6 0.1 convert_reduce_fusion
  13.7 0.1 copy.42
  13.8 0.2 reduce_window_sum.11
  14.0 0.1 copy.44
  14.1 0.0 copy-done.10
  14.1 0.1 select_reduce_fusion
  14.2 0.2 fusion.30
  14.3 0.2 copy.45
  14.5 0.0 copy-done.4
  14.5 0.9 convolution_convert_fusion.1
  15.4 0.2 fusion.7
  15.6 80.3 %all_to_all.25 = bf16[16,24,3712]{2,1,0:T(8,128)(2,1)} all-to-all(bf16[16,24,3712]{2,1,0:T(8,128)(2,1)S(1)} %fusion.7), channel_id=1, replica_groups=mesh['dp'=4,'grp'=16,'ylo'=2,'xhi'=2] {'grp'}, dimensions={0} | all-to-all | bytes 5701632 | tf_op jit(solution)/shard_map/all_to_all | solution.py:84
  95.9 0.0 all-gather.6.cloned.1.call-update
  96.0 1.1 copy-done.5
  97.1 5.1 %fusion.10 = (bf16[896,512]{1,0:T(8,128)(2,1)}, bf16[1,896,512]{2,1,0:T(8,128)(2,1)S(1)}, bf16[1,896,512]{2,1,0:T(8,128)(2,1)}) fusion(bf16[1,896,512]{2,1,0:T(8,128)(2,1)S(1)} %copy-done.5, bf16[896,512]{1,0:T(8,128)(2,1)} %reduce-scatter.2.cloned.1.call-done, f32[1,896,512]{2,1,0:T(8,128)} %param.16, f32[1,896,512]{2,1,0:T(8,128)} %param.17), kind=kLoop, calls=%fused_computation.22 | loop fusion | flops 8257536 | bytes 8257536 | tf_op jit(solution)/shard_map/convert_element_type | solution.py:25
  102.3 3.8 %all-to-all-start.1 = ((bf16[1,16,56,512]{3,2,0,1:T(8,128)(2,1)}), bf16[1,16,56,512]{3,2,0,1:T(8,128)(2,1)S(1)}, u32[]{:S(2)}, u32[]{:S(2)}) async-start(bf16[1,16,56,512]{3,2,0,1:T(8,128)(2,1)} %bitcast.125), calls=%async_computation.2 | async-start | bytes 1835008 | tf_op jit(solution)/shard_map/all_to_all | solution.py:32
  106.1 0.0 copy-done.1
  106.1 0.7 gather_fusion
  106.8 24.6 %all-to-all-done.1 = bf16[1,16,56,512]{3,2,0,1:T(8,128)(2,1)S(1)} async-done(((bf16[1,16,56,512]{3,2,0,1:T(8,128)(2,1)}), bf16[1,16,56,512]{3,2,0,1:T(8,128)(2,1)S(1)}, u32[]{:S(2)}, u32[]{:S(2)}) %all-to-all-start.1) | async-done | bytes 917536 | tf_op jit(solution)/shard_map/all_to_all | solution.py:32
  131.4 1.5 gather_fusion.1
  132.9 2.2 fusion.26
  135.2 3.8 %all-to-all-start.2 = ((bf16[1,16,56,512]{3,2,0,1:T(8,128)(2,1)}), bf16[1,16,56,512]{3,2,0,1:T(8,128)(2,1)S(1)}, u32[]{:S(2)}, u32[]{:S(2)}) async-start(bf16[1,16,56,512]{3,2,0,1:T(8,128)(2,1)} %fusion.26), calls=%async_computation.3 | async-start | bytes 1835008 | tf_op jit(solution)/shard_map/all_to_all | solution.py:34
  139.0 0.0 all-gather.4.cloned.1.call-start
  139.0 2.6 pad_maximum_fusion
  141.6 24.7 %all-to-all-done.2 = bf16[1,16,56,512]{3,2,0,1:T(8,128)(2,1)S(1)} async-done(((bf16[1,16,56,512]{3,2,0,1:T(8,128)(2,1)}), bf16[1,16,56,512]{3,2,0,1:T(8,128)(2,1)S(1)}, u32[]{:S(2)}, u32[]{:S(2)}) %all-to-all-start.2) | async-done | bytes 917536 | tf_op jit(solution)/shard_map/all_to_all | solution.py:34
  166.4 0.9 copy-done.2
  167.3 0.0 all-gather.4.cloned.1.call-update
  167.3 3.0 %copy.50 = bf16[2,16,56,512]{3,2,0,1:T(8,128)(2,1)} copy(bf16[2,16,56,512]{3,2,1,0:T(8,128)(2,1)} %bitcast.120) | data formatting | bytes 3670016 | tf_op jit(solution)/shard_map/reshape | solution.py:31
  170.3 3.7 %all-to-all-start.3 = ((bf16[2,16,56,512]{3,2,0,1:T(8,128)(2,1)}), bf16[2,16,56,512]{3,2,0,1:T(8,128)(2,1)S(1)}, u32[]{:S(2)}, u32[]{:S(2)}) async-start(bf16[2,16,56,512]{3,2,0,1:T(8,128)(2,1)} %copy.50), calls=%async_computation.4 | async-start | bytes 3670016 | tf_op jit(solution)/shard_map/all_to_all | solution.py:32
  174.0 45.9 %all-to-all-done.3 = bf16[2,16,56,512]{3,2,0,1:T(8,128)(2,1)S(1)} async-done(((bf16[2,16,56,512]{3,2,0,1:T(8,128)(2,1)}), bf16[2,16,56,512]{3,2,0,1:T(8,128)(2,1)S(1)}, u32[]{:S(2)}, u32[]{:S(2)}) %all-to-all-start.3) | async-done | bytes 1835040 | tf_op jit(solution)/shard_map/all_to_all | solution.py:32
  219.9 1.9 gather_fusion.2
  221.7 3.7 %all-to-all-start.4 = ((bf16[2,16,56,512]{3,2,0,1:T(8,128)(2,1)}), bf16[2,16,56,512]{3,2,0,1:T(8,128)(2,1)S(1)}, u32[]{:S(2)}, u32[]{:S(2)}) async-start(bf16[2,16,56,512]{3,2,0,1:T(8,128)(2,1)} %bitcast.121), calls=%async_computation.5 | async-start | bytes 3670016 | tf_op jit(solution)/shard_map/all_to_all | solution.py:34
  225.5 0.0 all-gather.6.cloned.1.call-done
  225.5 0.9 slice.57
  226.5 0.1 copy.53
  226.6 14.0 %all-gather.4.cloned.1.call-done = bf16[7168,512]{1,0:T(8,128)(2,1)} async-done(((bf16[896,512]{1,0:T(8,128)(2,1)}), bf16[7168,512]{1,0:T(8,128)(2,1)}) %all-gather.4.cloned.1.call-update) | async-done | bytes 7340048 | tf_op jit(solution)/shard_map/all_gather | solution.py:103
  240.6 6.3 %fusion.15 = f32[1,768,512]{2,1,0:T(8,128)S(1)} fusion(bf16[768,3712]{1,0:T(8,128)(2,1)} %bitcast.131, bf16[2,3584,512]{2,1,0:T(8,128)(2,1)} %bitcast.135), kind=kOutput, calls=%fused_computation.28 | convolution fusion | flops 2919235584 | bytes 14614528 | tf_op jit(solution)/shard_map/dot_general | solution.py:107
  246.9 0.0 copy-done.6
  247.0 1.2 copy-done.8
  248.1 3.1 %fusion.18 = f32[1,768,512]{2,1,0:T(8,128)S(1)} fusion(bf16[768,3712]{1,0:T(8,128)(2,1)S(1)} %bitcast.132, bf16[2,3584,512]{2,1,0:T(8,128)(2,1)S(1)} %bitcast.136), kind=kOutput, calls=%fused_computation.29 | convolution fusion | flops 2919235584 | bytes 14614528 | tf_op jit(solution)/shard_map/dot_general | solution.py:107
  251.2 0.4 fusion.14
  251.6 0.1 constant_dynamic-slice_fusion
  251.7 2.5 collective-permute-start
  254.3 17.5 %all-to-all-done.4 = bf16[2,16,56,512]{3,2,0,1:T(8,128)(2,1)S(1)} async-done(((bf16[2,16,56,512]{3,2,0,1:T(8,128)(2,1)}), bf16[2,16,56,512]{3,2,0,1:T(8,128)(2,1)S(1)}, u32[]{:S(2)}, u32[]{:S(2)}) %all-to-all-start.4) | async-done | bytes 1835040 | tf_op jit(solution)/shard_map/all_to_all | solution.py:34
  271.8 0.1 fusion.43
  271.9 1.5 convert.5
  273.4 1.5 convert.6
  274.8 0.0 collective-permute-done
  274.9 1.3 fusion.28
  276.2 1.0 copy.49
  277.1 0.0 copy-done.3
  277.1 0.9 copy.56
  (20 shorter events, 0.1 us)
Async XLA Ops:
  7.2 1.2 copy-start
  7.2 88.7 %reduce-scatter.2.cloned.1.call-start = ((), (), s32[]{:S(2)}) async-start(), calls=%async_computation.6 | async-start | bytes 4587520 | tf_op jit(solution)/shard_map/reduce_scatter | solution.py:85
  12.2 0.7 copy-start.9
  12.2 1.4 copy-start.7
  12.2 1.9 copy-start.10
  12.2 2.3 copy-start.4
  12.2 213.3 %all-gather.6.cloned.1.call-start = ((), (), s32[]{:S(2)}) async-start(), calls=%async_computation.8 | async-start | bytes 8552448 | tf_op jit(solution)/shard_map/all_gather | solution.py:95
  95.9 1.2 copy-start.5
  102.2 3.8 %copy-start.1 = (s32[16]{0:T(128)S(1)}, s32[16]{0:T(128)}, u32[]{:S(2)}) copy-start(s32[16]{0:T(128)} %param.22) | copy-start | bytes 196
  102.3 29.1 %all-to-all-start.1 = ((bf16[1,16,56,512]{3,2,0,1:T(8,128)(2,1)}), bf16[1,16,56,512]{3,2,0,1:T(8,128)(2,1)S(1)}, u32[]{:S(2)}, u32[]{:S(2)}) async-start(bf16[1,16,56,512]{3,2,0,1:T(8,128)(2,1)} %bitcast.125), calls=%async_computation.2 | async-start | bytes 1835008 | tf_op jit(solution)/shard_map/all_to_all | solution.py:32
  135.2 31.2 %all-to-all-start.2 = ((bf16[1,16,56,512]{3,2,0,1:T(8,128)(2,1)}), bf16[1,16,56,512]{3,2,0,1:T(8,128)(2,1)S(1)}, u32[]{:S(2)}, u32[]{:S(2)}) async-start(bf16[1,16,56,512]{3,2,0,1:T(8,128)(2,1)} %fusion.26), calls=%async_computation.3 | async-start | bytes 1835008 | tf_op jit(solution)/shard_map/all_to_all | solution.py:34
  139.0 101.6 %all-gather.4.cloned.1.call-start = ((), (), s32[]{:S(2)}) async-start(), calls=%async_computation.7 | async-start | bytes 8257536 | tf_op jit(solution)/shard_map/all_gather | solution.py:103
  166.4 0.9 copy-start.2
  170.3 49.6 %all-to-all-start.3 = ((bf16[2,16,56,512]{3,2,0,1:T(8,128)(2,1)}), bf16[2,16,56,512]{3,2,0,1:T(8,128)(2,1)S(1)}, u32[]{:S(2)}, u32[]{:S(2)}) async-start(bf16[2,16,56,512]{3,2,0,1:T(8,128)(2,1)} %copy.50), calls=%async_computation.4 | async-start | bytes 3670016 | tf_op jit(solution)/shard_map/all_to_all | solution.py:32
  221.7 50.0 %all-to-all-start.4 = ((bf16[2,16,56,512]{3,2,0,1:T(8,128)(2,1)}), bf16[2,16,56,512]{3,2,0,1:T(8,128)(2,1)S(1)}, u32[]{:S(2)}, u32[]{:S(2)}) async-start(bf16[2,16,56,512]{3,2,0,1:T(8,128)(2,1)} %bitcast.121), calls=%async_computation.5 | async-start | bytes 3670016 | tf_op jit(solution)/shard_map/all_to_all | solution.py:34
  240.6 6.3 %copy-start.6 = (bf16[32,24,3712]{2,1,0:T(8,128)(2,1)S(1)}, bf16[32,24,3712]{2,1,0:T(8,128)(2,1)}, u32[]{:S(2)}) copy-start(bf16[32,24,3712]{2,1,0:T(8,128)(2,1)} %all-gather.6.cloned.1.call-done) | copy-start | bytes 17104900
  240.6 7.5 %copy-start.8 = (bf16[7168,512]{1,0:T(8,128)(2,1)S(1)}, bf16[7168,512]{1,0:T(8,128)(2,1)}, u32[]{:S(2)}) copy-start(bf16[7168,512]{1,0:T(8,128)(2,1)} %all-gather.4.cloned.1.call-done) | copy-start | bytes 22020100
  251.7 23.1 %collective-permute-start = (bf16[768,256]{1,0:T(8,128)(2,1)S(1)}, bf16[768,256]{1,0:T(8,128)(2,1)}, u32[]{:S(2)}, u32[]{:S(2)}) collective-permute-start(bf16[768,256]{1,0:T(8,128)(2,1)S(1)} %get-tuple-element.30), channel_id=1, source_target_pairs={{0,1},{1,0},{2,3},{3,2},{4,5},{5,4},{6,7},{7,6},{8,9},{9,8},{10,11... | collective-permute-start | bytes 1179656 | tf_op jit(solution)/shard_map/ppermute | solution.py:118
  274.8 2.3 copy-start.3
Sparse Core Ops, SparseCore 0:
  12.3 45.8 reduce-scatter.1
  96.1 95.5 all-gather.5
  194.1 46.5 all-gather.3
where the time goes:
time: 285 us
  waiting for transfers between devices  127 us (45%)
  blocking collectives  80.3 us (28%)
  starting transfers between devices  17.7 us (6%)
  local copies, waits for them, and re-layouts  15.5 us (5%)
  other arithmetic  15.4 us (5%)
  between operations  14.6 us (5%)
  matrix products  14.2 us (5%)
    all_to_all x1, blocking collectives, local(): lax.all_to_all(payload, 'grp', split_axis=0, concat_axis=0, tiled=True)  80.3 us
    all_to_all x2, waiting for transfers between devices, migrate(): lax.all_to_all(split, 'grp', split_axis=1, concat_axis=1, tiled=True)  70.5 us
    all_to_all x2, waiting for transfers between devices, migrate(): lax.all_to_all(chosen, 'grp', split_axis=1, concat_axis=1, tiled=True)  42.2 us
    all_gather x1, waiting for transfers between devices, local(): both = lax.all_gather(new_weight, ('xhi', 'dp'), axis=0, tiled=True)  14 us
    dot_general x2, matrix products, local(): jnp.dot(near, both[k], preferred_element_type=jnp.float32)  9.38 us
    all_to_all x2, starting transfers between devices, migrate(): lax.all_to_all(chosen, 'grp', split_axis=1, concat_axis=1, tiled=True)  7.54 us
    all_to_all x2, starting transfers between devices, migrate(): lax.all_to_all(split, 'grp', split_axis=1, concat_axis=1, tiled=True)  7.49 us
    unnamed x24, local copies, waits for them, and re-layouts  6 us
  transfers between devices with their start and end apart: 8, of which 5 were waited for; matrix products, arithmetic and copies ran while one was open for 12% of the time, Pallas kernels for 0%

commit v1 on v0

--- a/solution.py
+++ b/solution.py
@@ -3,6 +3,7 @@
 from jax import lax
 from jax.sharding import Mesh
 from jax.sharding import PartitionSpec as P
+from jax.lax import all_to_all, axis_size
 
 D = 3584
 GRP = 4
@@ -63,6 +64,18 @@
     old_owner,
     new_owner,
 ):
+
+    def point_masks(arr_in):
+        return jnp.concatenate(
+            all_to_all(
+                jnp.stack(tuple((arr_in for _ in range(axis_size(("xhi", "dp")))))),
+                ("xhi", "dp"),
+                split_axis=0,
+                concat_axis=0,
+            ),
+            0,
+        )
+
     groups = lax.axis_size("grp")
     experts = groups * GRP
     token_slots = tokens.shape[2]
@@ -100,7 +113,7 @@
     moments = jnp.stack([first_next.astype(jnp.bfloat16), second_next.astype(jnp.bfloat16)])
     moments, new_weight = lax.optimization_barrier((moments, new_weight))
     moved = migrate(moments, group_source, groups, mode="clip")
-    both = lax.all_gather(new_weight, ("xhi", "dp"), axis=0, tiled=True)
+    both = point_masks(new_weight)
     both = both.reshape(2, -1, width)
     both = jnp.pad(both, ((0, 0), (0, SCALE_PAD), (0, 0)))
     projected = jnp.stack(

time: 285 us -> 373 us (1.31)
  blocking collectives: 80.3 us -> 131 us
  waiting for transfers between devices: 127 us -> 159 us
    all_to_all x0 -> x1, waiting for transfers between devices: none -> 77.2 us  [point_masks(): all_to_all(jnp.stack(tuple((arr_in for _ in range(axis_size(('xhi', 'dp')...]
    all_to_all x0 -> x1, blocking collectives: none -> 50.2 us  [migrate(): lax.all_to_all(split, 'grp', split_axis=1, concat_axis=1, tiled=True)]
    all_to_all x2 -> x1, waiting for transfers between devices: 70.5 us -> 24.6 us  [migrate(): lax.all_to_all(split, 'grp', split_axis=1, concat_axis=1, tiled=True)]
    all_gather x1 -> x0, waiting for transfers between devices: 14 us -> none  [local(): both = lax.all_gather(new_weight, ('xhi', 'dp'), axis=0, tiled=True)]
    ppermute x1, waiting for transfers between devices: 0.01 us -> 10.1 us  [local(): for_partner = lax.ppermute(other, 'xhi', perm=[(0, 1), (1, 0)])]
    all_to_all x0 -> x1, starting transfers between devices: none -> 5.23 us  [point_masks(): all_to_all(jnp.stack(tuple((arr_in for _ in range(axis_size(('xhi', 'dp')...]
    all_to_all x2, waiting for transfers between devices: 42.2 us -> 46.4 us  [migrate(): lax.all_to_all(chosen, 'grp', split_axis=1, concat_axis=1, tiled=True)]
    all_to_all x2 -> x1, starting transfers between devices: 7.49 us -> 3.77 us  [migrate(): lax.all_to_all(split, 'grp', split_axis=1, concat_axis=1, tiled=True)]
  transfers between devices with their start and end apart: 8 -> 7, of which waited for: 5 -> 5; matrix products, arithmetic and copies ran while one was open for 12% -> 6% of each run, Pallas kernels for 0% -> 0%
where the time goes in v1:
time: 373 us; the launch traced here: 371 us
  waiting for transfers between devices  159 us (43%)
  blocking collectives  131 us (35%)
  starting transfers between devices  19.4 us (5%)
  local copies, waits for them, and re-layouts  17.7 us (5%)
  matrix products  16.3 us (4%)
  between operations  14.9 us (4%)
  other arithmetic  13.2 us (4%)
    all_to_all x1, blocking collectives, local(): lax.all_to_all(payload, 'grp', split_axis=0, concat_axis=0, tiled=True)  80.4 us
    all_to_all x1, waiting for transfers between devices, point_masks(): all_to_all(jnp.stack(tuple((arr_in for _ in range(axis_size(('xhi', 'dp')...  77.2 us
    all_to_all x1, blocking collectives, migrate(): lax.all_to_all(split, 'grp', split_axis=1, concat_axis=1, tiled=True)  50.2 us
    all_to_all x2, waiting for transfers between devices, migrate(): lax.all_to_all(chosen, 'grp', split_axis=1, concat_axis=1, tiled=True)  46.4 us
    all_to_all x1, waiting for transfers between devices, migrate(): lax.all_to_all(split, 'grp', split_axis=1, concat_axis=1, tiled=True)  24.6 us
    dot_general x2, matrix products, local(): jnp.dot(near, both[k], preferred_element_type=jnp.float32)  11.4 us
    ppermute x1, waiting for transfers between devices, local(): for_partner = lax.ppermute(other, 'xhi', perm=[(0, 1), (1, 0)])  10.1 us
    all_to_all x2, starting transfers between devices, migrate(): lax.all_to_all(chosen, 'grp', split_axis=1, concat_axis=1, tiled=True)  8.17 us
  transfers between devices with their start and end apart: 7, of which 5 were waited for; matrix products, arithmetic and copies ran while one was open for 6% of the time, Pallas kernels for 0%

profile of v1, /device:TPU:6, one launch (start us, length us, event | category | flops | bytes accessed | tf_op | source)
XLA Modules:
  0.0 371.2 jit_solution(12327504678911778900)
XLA Ops:
  7.2 0.0 copy-start
  7.2 0.0 reduce-scatter.2.cloned.1.call-start
  7.2 1.1 copy-done
  8.4 3.8 %convolution_convert_fusion = bf16[3584,512]{1,0:T(8,128)(2,1)} fusion(bf16[1,1,128,3584]{3,2,1,0:T(8,128)(2,1)S(1)} %copy-done, bf16[1,1,128,512]{3,2,1,0:T(8,128)(2,1)} %param.14), kind=kOutput, calls=%fused_computation.5 | convolution fusion | flops 471597056 | bytes 4718592 | tf_op jit(solution)/shard_map/dot_general | solution.py:99
  12.2 0.0 copy-start.8
  12.2 0.0 copy-start.7
  12.2 0.0 copy-start.9
  12.2 0.0 reduce-scatter.2.cloned.1.call-update
  12.2 0.6 copy-done.8
  12.8 0.1 select_reduce_fusion.1
  13.6 0.0 copy-done.7
  13.6 0.1 convert_reduce_fusion
  13.7 0.1 copy.42
  13.8 0.2 reduce_window_sum.11
  14.0 0.1 copy.44
  14.1 0.0 copy-done.9
  14.1 0.1 select_reduce_fusion
  14.2 0.2 fusion.30
  14.3 0.2 copy.45
  14.5 0.0 copy-done.4
  14.5 0.9 convolution_convert_fusion.1
  15.4 0.2 fusion.7
  15.6 0.0 copy-start.5
  15.6 80.4 %all_to_all.30 = bf16[16,24,3712]{2,1,0:T(8,128)(2,1)} all-to-all(bf16[16,24,3712]{2,1,0:T(8,128)(2,1)S(1)} %fusion.7), channel_id=1, replica_groups=mesh['dp'=4,'grp'=16,'ylo'=2,'xhi'=2] {'grp'}, dimensions={0} | all-to-all | bytes 5701632 | tf_op jit(solution)/shard_map/all_to_all | solution.py:97
  96.1 0.0 copy-done.5
  96.1 5.1 %fusion.10 = (bf16[896,512]{1,0:T(8,128)(2,1)}, bf16[1,896,512]{2,1,0:T(8,128)(2,1)S(1)}, bf16[1,896,512]{2,1,0:T(8,128)(2,1)}) fusion(bf16[1,896,512]{2,1,0:T(8,128)(2,1)S(1)} %copy-done.5, bf16[896,512]{1,0:T(8,128)(2,1)} %reduce-scatter.2.cloned.1.call-done, f32[1,896,512]{2,1,0:T(8,128)} %param.16, f32[1,896,512]{2,1,0:T(8,128)} %param.17), kind=kLoop, calls=%fused_computation.22 | loop fusion | flops 8257536 | bytes 8257536 | tf_op jit(solution)/shard_map/convert_element_type | solution.py:26
  101.2 3.8 %all-to-all-start.1 = ((bf16[1,16,56,512]{3,2,0,1:T(8,128)(2,1)}), bf16[1,16,56,512]{3,2,0,1:T(8,128)(2,1)S(1)}, u32[]{:S(2)}, u32[]{:S(2)}) async-start(bf16[1,16,56,512]{3,2,0,1:T(8,128)(2,1)} %bitcast.125), calls=%async_computation.2 | async-start | bytes 1835008 | tf_op jit(solution)/shard_map/all_to_all | solution.py:33
  105.0 0.0 copy-done.2
  105.0 0.7 gather_fusion
  105.7 24.6 %all-to-all-done.1 = bf16[1,16,56,512]{3,2,0,1:T(8,128)(2,1)S(1)} async-done(((bf16[1,16,56,512]{3,2,0,1:T(8,128)(2,1)}), bf16[1,16,56,512]{3,2,0,1:T(8,128)(2,1)S(1)}, u32[]{:S(2)}, u32[]{:S(2)}) %all-to-all-start.1) | async-done | bytes 917536 | tf_op jit(solution)/shard_map/all_to_all | solution.py:33
  130.4 1.5 gather_fusion.1
  131.9 2.3 fusion.26
  134.2 3.8 %all-to-all-start.2 = ((bf16[1,16,56,512]{3,2,0,1:T(8,128)(2,1)}), bf16[1,16,56,512]{3,2,0,1:T(8,128)(2,1)S(1)}, u32[]{:S(2)}, u32[]{:S(2)}) async-start(bf16[1,16,56,512]{3,2,0,1:T(8,128)(2,1)} %fusion.26), calls=%async_computation.3 | async-start | bytes 1835008 | tf_op jit(solution)/shard_map/all_to_all | solution.py:35
  138.0 0.0 copy-done.3
  138.0 1.4 pad_maximum_fusion
  139.4 26.2 %all-to-all-done.2 = bf16[1,16,56,512]{3,2,0,1:T(8,128)(2,1)S(1)} async-done(((bf16[1,16,56,512]{3,2,0,1:T(8,128)(2,1)}), bf16[1,16,56,512]{3,2,0,1:T(8,128)(2,1)S(1)}, u32[]{:S(2)}, u32[]{:S(2)}) %all-to-all-start.2) | async-done | bytes 917536 | tf_op jit(solution)/shard_map/all_to_all | solution.py:35
  165.5 1.7 copy.50
  167.3 50.2 %all_to_all.31 = bf16[2,16,56,512]{3,2,0,1:T(8,128)(2,1)} all-to-all(bf16[2,16,56,512]{3,2,0,1:T(8,128)(2,1)S(1)} %copy.50), channel_id=1, replica_groups=mesh['dp'=4,'grp'=16,'ylo'=2,'xhi'=2] {'grp'}, dimensions={1} | all-to-all | bytes 3670016 | tf_op jit(solution)/shard_map/all_to_all | solution.py:33
  217.4 3.6 stack.46
  221.1 5.2 %all-to-all-start.3 = ((bf16[8,896,512]{2,1,0:T(8,128)(2,1)}), bf16[8,896,512]{2,1,0:T(8,128)(2,1)}, u32[]{:S(2)}, u32[]{:S(2)}) async-start(bf16[8,896,512]{2,1,0:T(8,128)(2,1)} %stack.46), calls=%async_computation.4 | async-start | bytes 14680064 | tf_op jit(solution)/shard_map/all_to_all | solution.py:70
  226.3 0.0 all-gather.3.cloned.1.call-start
  226.3 0.7 all-gather.3.cloned.1.call-update
  227.1 3.4 gather_fusion.2
  230.5 77.2 %all-to-all-done.3 = bf16[8,896,512]{2,1,0:T(8,128)(2,1)} async-done(((bf16[8,896,512]{2,1,0:T(8,128)(2,1)}), bf16[8,896,512]{2,1,0:T(8,128)(2,1)}, u32[]{:S(2)}, u32[]{:S(2)}) %all-to-all-start.3) | async-done | bytes 7340064 | tf_op jit(solution)/shard_map/all_to_all | solution.py:70
  307.7 4.4 %all-to-all-start.5 = ((bf16[2,16,56,512]{3,2,0,1:T(8,128)(2,1)}), bf16[2,16,56,512]{3,2,0,1:T(8,128)(2,1)}, u32[]{:S(2)}, u32[]{:S(2)}) async-start(bf16[2,16,56,512]{3,2,0,1:T(8,128)(2,1)} %bitcast.121), calls=%async_computation.6 | async-start | bytes 3670016 | tf_op jit(solution)/shard_map/all_to_all | solution.py:35
  312.1 0.0 all-gather.3.cloned.1.call-done
  312.2 0.9 slice.57
  313.1 0.1 copy.53
  313.3 0.0 copy-start.6
  313.3 6.3 %fusion.18 = f32[1,768,512]{2,1,0:T(8,128)S(1)} fusion(bf16[768,3712]{1,0:T(8,128)(2,1)} %bitcast.132, bf16[2,3584,512]{2,1,0:T(8,128)(2,1)} %bitcast.30), kind=kOutput, calls=%fused_computation.29 | convolution fusion | flops 2919235584 | bytes 14614528 | tf_op jit(solution)/shard_map/dot_general | solution.py:120
  319.6 0.0 copy-done.6
  319.6 5.1 %fusion.15 = f32[1,768,512]{2,1,0:T(8,128)S(1)} fusion(bf16[768,3712]{1,0:T(8,128)(2,1)S(1)} %bitcast.133, bf16[2,3584,512]{2,1,0:T(8,128)(2,1)} %bitcast.30), kind=kOutput, calls=%fused_computation.28 | convolution fusion | flops 2919235584 | bytes 14614528 | tf_op jit(solution)/shard_map/dot_general | solution.py:120
  324.7 0.4 fusion.14
  325.2 0.1 constant_dynamic-slice_fusion
  325.3 2.2 collective-permute-start
  327.4 10.1 %collective-permute-done = bf16[768,256]{1,0:T(8,128)(2,1)S(1)} collective-permute-done((bf16[768,256]{1,0:T(8,128)(2,1)S(1)}, bf16[768,256]{1,0:T(8,128)(2,1)S(1)}, u32[]{:S(2)}, u32[]{:S(2)}) %collective-permute-start) | collective-permute-done | bytes 393248 | tf_op jit(solution)/shard_map/ppermute | solution.py:131
  337.5 0.1 fusion.28
  337.6 1.0 copy.49
  338.6 20.3 %all-to-all-done.5 = bf16[2,16,56,512]{3,2,0,1:T(8,128)(2,1)} async-done(((bf16[2,16,56,512]{3,2,0,1:T(8,128)(2,1)}), bf16[2,16,56,512]{3,2,0,1:T(8,128)(2,1)}, u32[]{:S(2)}, u32[]{:S(2)}) %all-to-all-start.5) | async-done | bytes 1835040 | tf_op jit(solution)/shard_map/all_to_all | solution.py:35
  358.9 1.6 fusion.43
  360.5 1.5 convert.5
  361.9 1.5 convert.6
  363.4 0.9 copy.56
  364.3 0.0 copy-done.1
  (17 shorter events, 0.1 us)
Async XLA Ops:
  7.2 1.2 copy-start
  7.2 88.9 %reduce-scatter.2.cloned.1.call-start = ((), (), s32[]{:S(2)}) async-start(), calls=%async_computation.7 | async-start | bytes 4587520 | tf_op jit(solution)/shard_map/reduce_scatter | solution.py:98
  12.2 0.7 copy-start.8
  12.2 1.4 copy-start.7
  12.2 1.9 copy-start.9
  12.2 2.3 copy-start.4
  15.6 80.5 %copy-start.5 = (bf16[1,896,512]{2,1,0:T(8,128)(2,1)S(1)}, bf16[1,896,512]{2,1,0:T(8,128)(2,1)}, u32[]{:S(2)}) copy-start(bf16[1,896,512]{2,1,0:T(8,128)(2,1)} %param.15) | copy-start | bytes 2752516
  101.2 3.8 %copy-start.2 = (s32[16]{0:T(128)S(1)}, s32[16]{0:T(128)}, u32[]{:S(2)}) copy-start(s32[16]{0:T(128)} %param.22) | copy-start | bytes 196
  101.2 29.1 %all-to-all-start.1 = ((bf16[1,16,56,512]{3,2,0,1:T(8,128)(2,1)}), bf16[1,16,56,512]{3,2,0,1:T(8,128)(2,1)S(1)}, u32[]{:S(2)}, u32[]{:S(2)}) async-start(bf16[1,16,56,512]{3,2,0,1:T(8,128)(2,1)} %bitcast.125), calls=%async_computation.2 | async-start | bytes 1835008 | tf_op jit(solution)/shard_map/all_to_all | solution.py:33
  131.9 6.1 %copy-start.3 = (bf16[1,896,512]{2,1,0:T(8,128)(2,1)S(1)}, bf16[1,896,512]{2,1,0:T(8,128)(2,1)}, u32[]{:S(2)}) copy-start(bf16[1,896,512]{2,1,0:T(8,128)(2,1)} %get-tuple-element.26) | copy-start | bytes 2752516
  134.2 31.3 %all-to-all-start.2 = ((bf16[1,16,56,512]{3,2,0,1:T(8,128)(2,1)}), bf16[1,16,56,512]{3,2,0,1:T(8,128)(2,1)S(1)}, u32[]{:S(2)}, u32[]{:S(2)}) async-start(bf16[1,16,56,512]{3,2,0,1:T(8,128)(2,1)} %fusion.26), calls=%async_computation.3 | async-start | bytes 1835008 | tf_op jit(solution)/shard_map/all_to_all | solution.py:35
  221.1 86.6 %all-to-all-start.3 = ((bf16[8,896,512]{2,1,0:T(8,128)(2,1)}), bf16[8,896,512]{2,1,0:T(8,128)(2,1)}, u32[]{:S(2)}, u32[]{:S(2)}) async-start(bf16[8,896,512]{2,1,0:T(8,128)(2,1)} %stack.46), calls=%async_computation.4 | async-start | bytes 14680064 | tf_op jit(solution)/shard_map/all_to_all | solution.py:70
  226.3 85.8 %all-gather.3.cloned.1.call-start = ((), (), s32[]{:S(2)}) async-start(), calls=%async_computation.8 | async-start | bytes 8552448 | tf_op jit(solution)/shard_map/all_gather | solution.py:108
  307.7 51.2 %all-to-all-start.5 = ((bf16[2,16,56,512]{3,2,0,1:T(8,128)(2,1)}), bf16[2,16,56,512]{3,2,0,1:T(8,128)(2,1)}, u32[]{:S(2)}, u32[]{:S(2)}) async-start(bf16[2,16,56,512]{3,2,0,1:T(8,128)(2,1)} %bitcast.121), calls=%async_computation.6 | async-start | bytes 3670016 | tf_op jit(solution)/shard_map/all_to_all | solution.py:35
  313.3 6.3 %copy-start.6 = (bf16[32,24,3712]{2,1,0:T(8,128)(2,1)S(1)}, bf16[32,24,3712]{2,1,0:T(8,128)(2,1)}, u32[]{:S(2)}) copy-start(bf16[32,24,3712]{2,1,0:T(8,128)(2,1)} %all-gather.3.cloned.1.call-done) | copy-start | bytes 17104900
  325.3 12.3 %collective-permute-start = (bf16[768,256]{1,0:T(8,128)(2,1)S(1)}, bf16[768,256]{1,0:T(8,128)(2,1)S(1)}, u32[]{:S(2)}, u32[]{:S(2)}) collective-permute-start(bf16[768,256]{1,0:T(8,128)(2,1)S(1)} %get-tuple-element.30), channel_id=1, source_target_pairs={{0,1},{1,0},{2,3},{3,2},{4,5},{5,4},{6,7},{7,6},{8,9},{9,8},{10,11... | collective-permute-start | bytes 1179656 | tf_op jit(solution)/shard_map/ppermute | solution.py:131
  361.9 2.4 copy-start.1
Sparse Core Ops, SparseCore 0:
  12.3 45.8 reduce-scatter.1
  228.9 73.1 all-gather.2
